TPU v7x, 512 devices: a whole 4x8x8 slice. The times are simulated.
512 devices in a mesh: dp: 32 (over x, z_lo, core), ctx: 16 (over z_hi, y).
Axes of the slice: x: 4, y: 8, z: 8 (z_hi: 2, z_lo: 4; z = z_hi * 4 + z_lo), core: 2. Of those that a mesh axis runs over, the one named last changes fastest.
Arguments:
- queries: bfloat16 [32, 16, 128, 2048], P('dp', 'ctx'), may hold values from -2.5 to 2.5
- rotated_key_rows: bfloat16 [32, 16, 128, 512], P('dp', 'ctx'), may hold values from -2.5 to 2.5
- values: bfloat16 [32, 16, 128, 512], P('dp', 'ctx'), may hold values from -6 to 6
- cotangent: bfloat16 [32, 16, 128, 2048], P('dp', 'ctx'), may hold values from -6 to 6
- hidden: bfloat16 [32, 16, 128, 4096], P('dp', 'ctx'), may hold values from -6 to 6
- adapter_down_weight: bfloat16 [4096, 16], replicated, may hold values from -0.09375 to 0.09375
- adapter_up_weight: bfloat16 [16, 512], replicated, may hold values from -1.5 to 1.5
- segment_text_length: int32 [32, 16], P('dp', 'ctx'), may hold values from 19 to 78, as said below
Outputs:
- grad_queries: bfloat16 [32, 16, 128, 2048], P('dp', 'ctx')
- grad_keys: bfloat16 [32, 16, 128, 512], P('dp', 'ctx')
- grad_values: bfloat16 [32, 16, 128, 512], P('dp', 'ctx')
- grad_down: float32 [4096, 16], replicated
- grad_up: float32 [16, 512], replicated
Inputs may be any that keep to these rules, and one draw needn't show every extreme that they name: `segment_text_length`: every log has a segment with exactly 78 text tokens and another with the fewest.
All inputs are finite; a program needn't handle non-finite values.
Results may differ from a plain program's by a relative error of at most 0.0019.
The roundings to bfloat16 on the way count: a program that leaves them out, or rounds other values in their place, can miss the bound.
Values may be sent and summed in bfloat16 or wider, within the bound.
No kernel may reach another device: no remote copies, remote signals or barrier semaphores. Data moves between devices by JAX's collectives and lax.ppermute only.
A program may use at most 64 MiB of HBM per device.

v0:
```python
import math
import jax
import jax.numpy as jnp
from jax import lax
from jax.sharding import PartitionSpec as P

HEAD_SIZE = 128
SUMM = 50
adapter_scale = 2.0


def group_grads(query_group, key_group, value_group, cot_group, key_mask):
    softmax_scale = 1.0 / math.sqrt(HEAD_SIZE)
    scores = (
        jnp.einsum("tgd,md->gtm", query_group, key_group, preferred_element_type=jnp.float32)
        * softmax_scale
    )
    unnorm = jnp.exp(jnp.where(key_mask[None], scores, -jnp.inf))
    attend = unnorm / jnp.sum(unnorm, -1, keepdims=True)
    attend_grad = jnp.einsum(
        "tgd,md->gtm", cot_group, value_group, preferred_element_type=jnp.float32
    )
    row_dot = jnp.sum(attend * attend_grad, -1, keepdims=True)
    dscore = (attend * (attend_grad - row_dot)).astype(jnp.bfloat16)
    attend_low = attend.astype(jnp.bfloat16)
    query_grad = (
        jnp.einsum("gtm,md->tgd", dscore, key_group, preferred_element_type=jnp.float32)
        * softmax_scale
    )
    key_grad = (
        jnp.einsum("gtm,tgd->md", dscore, query_group, preferred_element_type=jnp.float32)
        * softmax_scale
    )
    value_grad = jnp.einsum(
        "gtm,tgd->md", attend_low, cot_group, preferred_element_type=jnp.float32
    )
    return (query_grad, key_grad, value_grad)


def adapter_terms(hidden_piece, low_rank_piece, value_piece, adapter_up_weight):
    contract = (((0,), (0,)), ((), ()))
    backward_step = lax.dot_general(
        value_piece, adapter_up_weight, (((1,), (1,)), ((), ())), preferred_element_type=jnp.float32
    ).astype(jnp.bfloat16)
    down_part = lax.dot_general(
        hidden_piece, backward_step, contract, preferred_element_type=jnp.float32
    )
    up_part = lax.dot_general(
        low_rank_piece, value_piece, contract, preferred_element_type=jnp.float32
    )
    return (down_part, up_part)


def per_device(
    queries,
    rotated_key_rows,
    values,
    cotangent,
    hidden,
    adapter_down_weight,
    adapter_up_weight,
    segment_text_length,
):
    query_rows = queries[0, 0]
    key_local = rotated_key_rows[0, 0]
    value_local = values[0, 0]
    cot_rows = cotangent[0, 0]
    hidden_row_block = hidden[0, 0]
    length = segment_text_length[0, 0]
    position = lax.axis_index("ctx")
    segment_list = lax.axis_size("ctx")
    log_batch = lax.axis_size("dp")
    tokens = query_rows.shape[0]
    width = key_local.shape[1]
    kv_heads = width // HEAD_SIZE
    groups = query_rows.shape[1] // width
    live = length + SUMM
    rows = jnp.arange(tokens)
    cot_rows = jnp.where((rows < live)[:, None], cot_rows, jnp.zeros_like(cot_rows))
    own_keys = lax.dynamic_slice_in_dim(key_local, length, SUMM, 0)
    own_values = lax.dynamic_slice_in_dim(value_local, length, SUMM, 0)
    memory_keys, memory_values = (
        lax.all_gather(own_keys, "ctx", axis=0, tiled=True),
        lax.all_gather(own_values, "ctx", axis=0, tiled=True),
    )
    count = memory_keys.shape[0]
    memory_owner = jnp.arange(count) // SUMM
    local_mask = (rows[None, :] <= rows[:, None]) & (rows[None, :] < live)
    memory_mask = jnp.broadcast_to((memory_owner < position)[None, :], (tokens, count))
    key_mask = jnp.concatenate([memory_mask, local_mask], axis=1)
    all_keys = jnp.concatenate([memory_keys, key_local], 0)
    all_values = jnp.concatenate([memory_values, value_local], 0)
    query_parts, key_parts, value_parts = ([], [], [])
    for group in range(kv_heads):
        qcols = slice(group * groups * HEAD_SIZE, (group + 1) * groups * HEAD_SIZE)
        kcols = slice(group * HEAD_SIZE, (group + 1) * HEAD_SIZE)
        query_grad, key_grad, value_grad = group_grads(
            query_rows[:, qcols].reshape(tokens, groups, HEAD_SIZE),
            all_keys[:, kcols],
            all_values[:, kcols],
            cot_rows[:, qcols].reshape(tokens, groups, HEAD_SIZE),
            key_mask,
        )
        query_parts.append(query_grad.reshape(tokens, groups * HEAD_SIZE))
        key_parts.append(key_grad)
        value_parts.append(value_grad)
    query_out = jnp.concatenate(query_parts, 1).astype(jnp.bfloat16)
    key_grad = jnp.concatenate(key_parts, 1)
    value_grad = jnp.concatenate(value_parts, 1)
    memory_key_grad, local_key = (key_grad[:count], key_grad[count:])
    memory_value_grad, local_value = (value_grad[:count], value_grad[count:])
    back_key, back_value = (
        lax.psum_scatter(memory_key_grad, "ctx", scatter_dimension=0, tiled=True),
        lax.psum_scatter(memory_value_grad, "ctx", scatter_dimension=0, tiled=True),
    )
    key_out = (
        local_key + lax.dynamic_update_slice_in_dim(jnp.zeros_like(local_key), back_key, length, 0)
    ).astype(jnp.bfloat16)
    value_result = (
        local_value
        + lax.dynamic_update_slice_in_dim(jnp.zeros_like(local_value), back_value, length, 0)
    ).astype(jnp.bfloat16)
    low_rank_rows = jnp.dot(
        hidden_row_block, adapter_down_weight, preferred_element_type=jnp.float32
    ).astype(jnp.bfloat16)
    down_sum, up_sum = lax.psum(
        adapter_terms(hidden_row_block, low_rank_rows, value_result, adapter_up_weight),
        ("dp", "ctx"),
    )
    adapter_factor = adapter_scale / (log_batch * segment_list)
    return (
        query_out[None, None],
        key_out[None, None],
        value_result[None, None],
        down_sum * adapter_factor,
        up_sum * adapter_factor,
    )


def solution(mesh):
    placed = (
        P("dp", "ctx", None, None),
        P("dp", "ctx", None, None),
        P("dp", "ctx", None, None),
        P("dp", "ctx", None, None),
        P("dp", "ctx", None, None),
        P(),
        P(),
        P("dp", "ctx"),
    )
    return jax.shard_map(
        per_device,
        mesh=mesh,
        in_specs=placed,
        out_specs=(
            P("dp", "ctx", None, None),
            P("dp", "ctx", None, None),
            P("dp", "ctx", None, None),
            P(),
            P(),
        ),
        check_vma=False,
    )
```

profile of v0, /device:TPU:23, one launch (start us, length us, event | category | flops | bytes accessed | tf_op | source)
XLA Modules:
  0.0 690.2 jit_solution(10573385685993678899)
XLA Ops:
  12.5 56.8 %all-gather.1 = bf16[1,1,800,512]{3,1,0,2:T(2,128)(2,1)S(1)} all-gather(bf16[1,1,50,512]{3,1,0,2:T(2,128)(2,1)S(1)} %copy.106), channel_id=3, replica_groups=mesh['dp'=32,'ctx'=16] {'ctx'}, dimensions={2}, use_global_device_ids=true | all-gather | bytes 870400 | tf_op jit(solution)/shard_map/all_gather | solution.py:84
  69.5 58.1 %all-gather = bf16[1,1,800,512]{3,1,0,2:T(2,128)(2,1)S(1)} all-gather(bf16[1,1,50,512]{3,1,0,2:T(2,128)(2,1)S(1)} %copy.105), channel_id=2, replica_groups=mesh['dp'=32,'ctx'=16] {'ctx'}, dimensions={2}, use_global_device_ids=true | all-gather | bytes 870400 | tf_op jit(solution)/shard_map/all_gather | solution.py:83
  127.8 1.7 fusion.48
  129.5 1.6 fusion.52
  131.1 1.7 fusion.61
  132.8 1.6 fusion.44
  134.7 3.7 fusion.6
  138.4 2.1 convolution_bitcast_fusion.2
  140.5 1.8 fusion.8
  144.6 4.1 fusion.2
  148.7 2.9 convolution_bitcast_fusion.1
  151.6 1.8 fusion.4
  154.6 4.3 fusion.10
  158.9 2.9 convolution_bitcast_fusion.3
  161.8 1.8 fusion.12
  165.8 4.2 fusion.14
  170.0 2.1 convolution_bitcast_fusion.4
  172.2 2.0 fusion.16
  175.7 1.9 pad_maximum_fusion
  177.5 77.3 %fusion.89 = (f32[56,512]{1,0:T(8,128)}, f32[56,512]{1,0:T(8,128)}) fusion(f32[800,512]{1,0:T(8,128)} %get-tuple-element.26, f32[800,512]{1,0:T(8,128)} %get-tuple-element.25), kind=kCustom, calls=%all-reduce-scatter.2 | all-reduce-scatter fusion | flops 917505 | bytes 3508224
  254.8 2.0 collective-permute-start.2
  258.4 1.9 collective-permute-start.3
  260.3 1.9 collective-permute-start
  263.8 12.0 %collective-permute-start.1 = (f32[34,512]{1,0:T(8,128)}, f32[34,512]{1,0:T(8,128)}, u32[]{:S(2)}, u32[]{:S(2)}) collective-permute-start(f32[34,512]{1,0:T(8,128)} %slice.106), channel_id=1, source_target_pairs={{0,2},{1,3},{2,4},{3,5},{4,6},{5,7},{6,8},{7,9},{8,10},{9,11},{10,... | collective-permute-start | bytes 208904
  275.7 2.2 fusion.24
  283.8 1.7 copy.75
  287.4 1.8 pad_maximum_fusion.6
  289.3 2.8 concatenate.44
  293.7 2.8 concatenate.45
  298.6 116.7 %psum.15 = f32[16,512]{1,0:T(8,128)S(1)} all-reduce(f32[16,512]{1,0:T(8,128)S(1)} %fusion.26), channel_id=1, replica_groups=mesh['dp'=32,'ctx'=16] {'dp','ctx'}, use_global_device_ids=true, to_apply=%region_11.12 | all-reduce | flops 8192 | bytes 65536 | tf_op jit(solution)/shard_map/psum | solution.py:126
  417.1 264.6 %all-reduce.7.cloned.1.call-done = f32[4096,16]{0,1:T(8,128)} async-done(((f32[4096,16]{0,1:T(8,128)}), f32[4096,16]{0,1:T(8,128)}) %all-reduce.7.cloned.1.call-update) | async-done | bytes 262160 | tf_op jit(solution)/shard_map/psum | solution.py:126
  681.7 1.7 broadcast_multiply_fusion
  (131 shorter events, 27.7 us)
Async XLA Ops:
  7.2 290.9 %copy-start = (bf16[1,1,128,4096]{3,2,1,0:T(8,128)(2,1)S(1)}, bf16[1,1,128,4096]{3,2,1,0:T(8,128)(2,1)}, u32[]{:S(2)}) copy-start(bf16[1,1,128,4096]{3,2,1,0:T(8,128)(2,1)} %param.12) | copy-start | bytes 3145732
  7.2 4.9 copy-start.31
  7.2 674.5 %all-reduce.7.cloned.1.call-start = ((), (), s32[]{:S(2)}) async-start(), calls=%async_computation | async-start | bytes 524288 | tf_op jit(solution)/shard_map/psum | solution.py:126
  12.1 132.5 %copy-start.34 = (bf16[128,512]{0,1:T(8,128)(2,1)}, bf16[128,512]{0,1:T(8,128)(2,1)S(1)}, u32[]{:S(2)}) copy-start(bf16[128,512]{0,1:T(8,128)(2,1)S(1)} %get-tuple-element.14) | copy-start | bytes 393220
  12.5 117.0 %copy-start.26 = (bf16[128,512]{0,1:T(8,128)(2,1)}, bf16[128,512]{0,1:T(8,128)(2,1)S(1)}, u32[]{:S(2)}) copy-start(bf16[128,512]{0,1:T(8,128)(2,1)S(1)} %get-tuple-element.12) | copy-start | bytes 393220
  69.5 58.3 %copy-start.24 = (bf16[1,1,128,512]{3,2,1,0:T(8,128)(2,1)S(1)}, bf16[1,1,128,512]{3,2,1,0:T(8,128)(2,1)}, u32[]{:S(2)}) copy-start(bf16[1,1,128,512]{3,2,1,0:T(8,128)(2,1)} %param.10) | copy-start | bytes 393220
  134.7 9.9 %copy-start.37 = (pred[128,928]{0,1:T(8,128)(4,1)}, pred[128,928]{0,1:T(8,128)(4,1)S(1)}, u32[]{:S(2)}) copy-start(pred[128,928]{0,1:T(8,128)(4,1)S(1)} %pad_add_fusion) | copy-start | bytes 356356
  134.7 9.9 %copy-start.27 = (bf16[928,128,1]{1,0,2:T(8,128)(2,1)}, bf16[928,128,1]{1,0,2:T(8,128)(2,1)S(1)}, u32[]{:S(2)}) copy-start(bf16[928,128,1]{1,0,2:T(8,128)(2,1)S(1)} %fusion.64) | copy-start | bytes 712708
  148.7 2.9 copy-start.8
  148.7 2.9 copy-start.40
  158.9 2.9 copy-start.7
  158.9 2.9 copy-start.41
  161.8 2.8 copy-start.33
  170.0 2.1 copy-start.39
  172.1 3.5 copy-start.14
  172.1 3.1 copy-start.32
  172.1 3.5 copy-start.10
  172.1 3.5 copy-start.12
  172.2 3.5 copy-start.16
  172.2 3.5 copy-start.18
  172.2 3.5 copy-start.20
  254.8 23.1 %copy-start.28 = (bf16[928,128,1]{1,0,2:T(8,128)(2,1)S(1)}, bf16[928,128,1]{1,0,2:T(8,128)(2,1)}, u32[]{:S(2)}) copy-start(bf16[928,128,1]{1,0,2:T(8,128)(2,1)} %copy-done.27) | copy-start | bytes 712708
  254.8 24.1 %copy-start.3 = (bf16[4,128,928]{1,2,0:T(8,128)(2,1)S(1)}, bf16[4,128,928]{1,2,0:T(8,128)(2,1)}, u32[]{:S(2)}) copy-start(bf16[4,128,928]{1,2,0:T(8,128)(2,1)} %copy-done.2) | copy-start | bytes 2850820
  254.8 38.9 %collective-permute-start.2 = (f32[56,512]{1,0:T(8,128)}, f32[56,512]{1,0:T(8,128)}, u32[]{:S(2)}, u32[]{:S(2)}) collective-permute-start(f32[56,512]{1,0:T(8,128)} %get-tuple-element.8), channel_id=1, source_target_pairs={{0,1},{1,2},{2,3},{3,4},{4,5},{5,6},{6,7},{7,8},{8,9},{9,10},{10,1... | collective-permute-start | bytes 344072
  258.4 35.3 %collective-permute-start.3 = (f32[34,512]{1,0:T(8,128)}, f32[34,512]{1,0:T(8,128)}, u32[]{:S(2)}, u32[]{:S(2)}) collective-permute-start(f32[34,512]{1,0:T(8,128)} %slice.107), channel_id=1, source_target_pairs={{0,2},{1,3},{2,4},{3,5},{4,6},{5,7},{6,8},{7,9},{8,10},{9,11},{10,... | collective-permute-start | bytes 208904
  260.3 28.9 %collective-permute-start = (f32[56,512]{1,0:T(8,128)}, f32[56,512]{1,0:T(8,128)}, u32[]{:S(2)}, u32[]{:S(2)}) collective-permute-start(f32[56,512]{1,0:T(8,128)} %get-tuple-element.7), channel_id=1, source_target_pairs={{0,1},{1,2},{2,3},{3,4},{4,5},{5,6},{6,7},{7,8},{8,9},{9,10},{10,1... | collective-permute-start | bytes 344072
  263.8 25.5 %collective-permute-start.1 = (f32[34,512]{1,0:T(8,128)}, f32[34,512]{1,0:T(8,128)}, u32[]{:S(2)}, u32[]{:S(2)}) collective-permute-start(f32[34,512]{1,0:T(8,128)} %slice.106), channel_id=1, source_target_pairs={{0,2},{1,3},{2,4},{3,5},{4,6},{5,7},{6,8},{7,9},{8,10},{9,11},{10,... | collective-permute-start | bytes 208904
  281.0 8.2 %copy-start.11 = (f32[928,128]{1,0:T(8,128)S(1)}, f32[928,128]{1,0:T(8,128)}, u32[]{:S(2)}) copy-start(f32[928,128]{1,0:T(8,128)} %convolution_bitcast_fusion.1) | copy-start | bytes 1425412
  281.0 8.2 %copy-start.13 = (f32[928,128]{1,0:T(8,128)S(1)}, f32[928,128]{1,0:T(8,128)}, u32[]{:S(2)}) copy-start(f32[928,128]{1,0:T(8,128)} %convolution_bitcast_fusion.3) | copy-start | bytes 1425412
  281.0 8.2 %copy-start.15 = (f32[928,128]{1,0:T(8,128)S(1)}, f32[928,128]{1,0:T(8,128)}, u32[]{:S(2)}) copy-start(f32[928,128]{1,0:T(8,128)} %copy-done.14) | copy-start | bytes 1425412
  289.2 8.9 %copy-start.36 = (bf16[4096,16]{0,1:T(8,128)(2,1)S(1)}, bf16[4096,16]{0,1:T(8,128)(2,1)}, u32[]{:S(2)}) copy-start(bf16[4096,16]{0,1:T(8,128)(2,1)} %param.13) | copy-start | bytes 393220
  292.2 123.2 %copy-start.38 = (bf16[16,512]{1,0:T(8,128)(2,1)S(1)}, bf16[16,512]{1,0:T(8,128)(2,1)}, u32[]{:S(2)}) copy-start(bf16[16,512]{1,0:T(8,128)(2,1)} %param.14) | copy-start | bytes 49156
  (15 other events, 25.5 us)
Sparse Core Ops, SparseCore 0:
  416.6 265.0 all-reduce.6
where the time goes:
time: 691 us; the launch traced here: 690 us
  blocking collectives  309 us (45%)
  waiting for transfers between devices  265 us (38%)
  matrix products  43.7 us (6%)
  local copies, waits for them, and re-layouts  23.8 us (3%)
  starting transfers between devices  17.9 us (3%)
  between operations  16 us (2%)
  other arithmetic  15.3 us (2%)
    psum x1, waiting for transfers between devices, per_device(): lax.psum(adapter_terms(hidden_row_block, low_rank_rows, value_result, ada...  265 us
    psum x1, blocking collectives, per_device(): lax.psum(adapter_terms(hidden_row_block, low_rank_rows, value_result, ada...  117 us
    unnamed x1, blocking collectives  77.3 us
    all_gather x1, blocking collectives, per_device(): lax.all_gather(own_keys, 'ctx', axis=0, tiled=True)  58.1 us
    all_gather x1, blocking collectives, per_device(): lax.all_gather(own_values, 'ctx', axis=0, tiled=True)  56.8 us
    unnamed x4, starting transfers between devices  17.8 us
    div x4, matrix products, group_grads(): attend = unnorm / jnp.sum(unnorm, -1, keepdims=True)  16.4 us
    unnamed x95, local copies, waits for them, and re-layouts  16.1 us
  transfers between devices with their start and end apart: 5, of which 1 were waited for; matrix products, arithmetic and copies ran while one was open for 3% of the time, Pallas kernels for 0%

commit v1 on v0

--- a/solution.py
+++ b/solution.py
@@ -7,6 +7,11 @@
 HEAD_SIZE = 128
 SUMM = 50
 adapter_scale = 2.0
+
+
+def axis_by_axis(array, first, second):
+    partial = lax.psum(array, first)
+    return lax.psum(partial, second)
 
 
 def group_grads(query_group, key_group, value_group, cot_group, key_mask):
@@ -123,9 +128,8 @@
     low_rank_rows = jnp.dot(
         hidden_row_block, adapter_down_weight, preferred_element_type=jnp.float32
     ).astype(jnp.bfloat16)
-    down_sum, up_sum = lax.psum(
-        adapter_terms(hidden_row_block, low_rank_rows, value_result, adapter_up_weight),
-        ("dp", "ctx"),
+    down_sum, up_sum = axis_by_axis(
+        adapter_terms(hidden_row_block, low_rank_rows, value_result, adapter_up_weight), "dp", "ctx"
     )
     adapter_factor = adapter_scale / (log_batch * segment_list)
     return (

time: 691 us -> 1020 us (1.48)
  the two profiles are of different devices: /device:TPU:23 before, /device:TPU:2 now
where the time goes in v1:
time: 1020 us
  waiting for transfers between devices  485 us (48%)
  blocking collectives  426 us (42%)
  matrix products  44.6 us (4%)
  local copies, waits for them, and re-layouts  23.3 us (2%)
  between operations  16 us (2%)
  other arithmetic  15.3 us (2%)
    psum x1, waiting for transfers between devices, axis_by_axis(): partial = lax.psum(array, first)  276 us
    psum x1, waiting for transfers between devices, axis_by_axis(): return lax.psum(partial, second)  208 us
    psum x1, blocking collectives, axis_by_axis(): partial = lax.psum(array, first)  114 us
    psum x1, blocking collectives, axis_by_axis(): return lax.psum(partial, second)  92.2 us
    unnamed x1, blocking collectives  84.7 us
    all_gather x1, blocking collectives, per_device(): lax.all_gather(own_values, 'ctx', axis=0, tiled=True)  73.4 us
    all_gather x1, blocking collectives, per_device(): lax.all_gather(own_keys, 'ctx', axis=0, tiled=True)  62.4 us
  transfers between devices with their start and end apart: 6, of which 2 were waited for; matrix products, arithmetic and copies ran while one was open for 3% of the time, Pallas kernels for 0%

profile of v1, /device:TPU:2, one launch (start us, length us, event | category | flops | bytes accessed | tf_op | source)
XLA Modules:
  0.0 1019.6 jit_solution(14762377911569580545)
XLA Ops:
  12.4 73.4 %all-gather.1 = bf16[1,1,800,512]{3,1,0,2:T(2,128)(2,1)S(1)} all-gather(bf16[1,1,50,512]{3,1,0,2:T(2,128)(2,1)S(1)} %copy.106), channel_id=3, replica_groups=mesh['dp'=32,'ctx'=16] {'ctx'}, dimensions={2}, use_global_device_ids=true | all-gather | bytes 870400 | tf_op jit(solution)/shard_map/all_gather | solution.py:89
  86.0 62.4 %all-gather = bf16[1,1,800,512]{3,1,0,2:T(2,128)(2,1)S(1)} all-gather(bf16[1,1,50,512]{3,1,0,2:T(2,128)(2,1)S(1)} %copy.105), channel_id=2, replica_groups=mesh['dp'=32,'ctx'=16] {'ctx'}, dimensions={2}, use_global_device_ids=true | all-gather | bytes 870400 | tf_op jit(solution)/shard_map/all_gather | solution.py:88
  148.7 1.7 fusion.48
  152.0 1.7 fusion.61
  155.6 3.7 fusion.6
  159.3 2.1 convolution_bitcast_fusion.2
  161.4 1.8 fusion.8
  165.4 4.1 fusion.2
  169.5 2.9 convolution_bitcast_fusion.1
  172.5 1.8 fusion.4
  175.5 4.3 fusion.10
  179.8 2.9 convolution_bitcast_fusion.3
  182.7 1.8 fusion.12
  186.6 4.2 fusion.14
  190.9 2.1 convolution_bitcast_fusion.4
  193.0 2.0 fusion.16
  196.5 1.9 pad_maximum_fusion
  198.4 84.7 %fusion.89 = (f32[56,512]{1,0:T(8,128)}, f32[56,512]{1,0:T(8,128)}) fusion(f32[800,512]{1,0:T(8,128)} %get-tuple-element.26, f32[800,512]{1,0:T(8,128)} %get-tuple-element.25), kind=kCustom, calls=%all-reduce-scatter.2 | all-reduce-scatter fusion | flops 917505 | bytes 3508224
  283.1 3.6 collective-permute-start.2
  288.2 1.9 collective-permute-start.3
  290.1 1.9 collective-permute-start
  293.6 1.9 collective-permute-start.1
  295.5 2.2 fusion.24
  303.5 1.7 copy.75
  307.1 1.8 pad_maximum_fusion.6
  309.0 2.8 concatenate.45
  313.9 113.9 %psum.30 = f32[16,512]{1,0:T(8,128)S(1)} all-reduce(f32[16,512]{1,0:T(8,128)S(1)} %fusion.26), channel_id=1, replica_groups=mesh['dp'=32,'ctx'=16] {'dp'}, use_global_device_ids=true, to_apply=%region_12.13 | all-reduce | flops 8192 | bytes 65536 | tf_op jit(solution)/shard_map/psum | solution.py:13
  427.8 92.2 %psum.31 = f32[16,512]{1,0:T(8,128)S(1)} all-reduce(f32[16,512]{1,0:T(8,128)S(1)} %psum.30), channel_id=1, replica_groups=mesh['dp'=32,'ctx'=16] {'ctx'}, use_global_device_ids=true, to_apply=%region_13.14 | all-reduce | flops 8192 | bytes 65536 | tf_op jit(solution)/shard_map/psum | solution.py:14
  521.8 2.8 concatenate.44
  525.3 276.4 %all-reduce.8.cloned.1.call-done = f32[4096,16]{0,1:T(8,128)} async-done(((f32[4096,16]{0,1:T(8,128)}), f32[4096,16]{0,1:T(8,128)}) %all-reduce.8.cloned.1.call-update) | async-done | bytes 262160 | tf_op jit(solution)/shard_map/psum | solution.py:13
  803.1 208.0 %all-reduce.10.cloned.1.call-done = f32[4096,16]{0,1:T(8,128)} async-done(((f32[4096,16]{0,1:T(8,128)}), f32[4096,16]{0,1:T(8,128)}) %all-reduce.10.cloned.1.call-update) | async-done | bytes 262160 | tf_op jit(solution)/shard_map/psum | solution.py:14
  1011.1 1.7 broadcast_multiply_fusion
  (133 shorter events, 31.4 us)
Async XLA Ops:
  7.2 305.3 %copy-start = (bf16[1,1,128,4096]{3,2,1,0:T(8,128)(2,1)S(1)}, bf16[1,1,128,4096]{3,2,1,0:T(8,128)(2,1)}, u32[]{:S(2)}) copy-start(bf16[1,1,128,4096]{3,2,1,0:T(8,128)(2,1)} %param.12) | copy-start | bytes 3145732
  7.2 4.9 copy-start.31
  7.2 794.6 %all-reduce.8.cloned.1.call-start = ((), (), s32[]{:S(2)}) async-start(), calls=%async_computation | async-start | bytes 524288 | tf_op jit(solution)/shard_map/psum | solution.py:13
  12.1 153.4 %copy-start.34 = (bf16[128,512]{0,1:T(8,128)(2,1)}, bf16[128,512]{0,1:T(8,128)(2,1)S(1)}, u32[]{:S(2)}) copy-start(bf16[128,512]{0,1:T(8,128)(2,1)S(1)} %get-tuple-element.14) | copy-start | bytes 393220
  12.4 137.9 %copy-start.26 = (bf16[128,512]{0,1:T(8,128)(2,1)}, bf16[128,512]{0,1:T(8,128)(2,1)S(1)}, u32[]{:S(2)}) copy-start(bf16[128,512]{0,1:T(8,128)(2,1)S(1)} %get-tuple-element.12) | copy-start | bytes 393220
  86.0 62.7 %copy-start.24 = (bf16[1,1,128,512]{3,2,1,0:T(8,128)(2,1)S(1)}, bf16[1,1,128,512]{3,2,1,0:T(8,128)(2,1)}, u32[]{:S(2)}) copy-start(bf16[1,1,128,512]{3,2,1,0:T(8,128)(2,1)} %param.10) | copy-start | bytes 393220
  155.5 9.9 copy-start.36
  155.6 9.9 copy-start.27
  169.5 2.9 copy-start.8
  169.5 2.9 copy-start.39
  179.8 2.9 copy-start.7
  179.8 2.9 copy-start.40
  182.6 2.8 copy-start.33
  190.8 2.1 copy-start.38
  192.9 3.5 copy-start.14
  193.0 3.0 copy-start.32
  193.0 3.5 copy-start.10
  193.0 3.5 copy-start.12
  193.0 3.5 copy-start.16
  193.0 3.5 copy-start.18
  193.0 3.5 copy-start.20
  283.0 14.6 %copy-start.28 = (bf16[928,128,1]{1,0,2:T(8,128)(2,1)S(1)}, bf16[928,128,1]{1,0,2:T(8,128)(2,1)}, u32[]{:S(2)}) copy-start(bf16[928,128,1]{1,0,2:T(8,128)(2,1)} %copy-done.27) | copy-start | bytes 712708
  283.0 15.6 %copy-start.3 = (bf16[4,128,928]{1,2,0:T(8,128)(2,1)S(1)}, bf16[4,128,928]{1,2,0:T(8,128)(2,1)}, u32[]{:S(2)}) copy-start(bf16[4,128,928]{1,2,0:T(8,128)(2,1)} %copy-done.2) | copy-start | bytes 2850820
  283.1 26.0 %collective-permute-start.2 = (f32[56,512]{1,0:T(8,128)}, f32[56,512]{1,0:T(8,128)}, u32[]{:S(2)}, u32[]{:S(2)}) collective-permute-start(f32[56,512]{1,0:T(8,128)} %get-tuple-element.8), channel_id=1, source_target_pairs={{0,1},{1,2},{2,3},{3,4},{4,5},{5,6},{6,7},{7,8},{8,9},{9,10},{10,1... | collective-permute-start | bytes 344072
  288.2 20.8 %collective-permute-start.3 = (f32[34,512]{1,0:T(8,128)}, f32[34,512]{1,0:T(8,128)}, u32[]{:S(2)}, u32[]{:S(2)}) collective-permute-start(f32[34,512]{1,0:T(8,128)} %slice.107), channel_id=1, source_target_pairs={{0,2},{1,3},{2,4},{3,5},{4,6},{5,7},{6,8},{7,9},{8,10},{9,11},{10,... | collective-permute-start | bytes 208904
  290.1 231.7 %collective-permute-start = (f32[56,512]{1,0:T(8,128)}, f32[56,512]{1,0:T(8,128)}, u32[]{:S(2)}, u32[]{:S(2)}) collective-permute-start(f32[56,512]{1,0:T(8,128)} %get-tuple-element.7), channel_id=1, source_target_pairs={{0,1},{1,2},{2,3},{3,4},{4,5},{5,6},{6,7},{7,8},{8,9},{9,10},{10,1... | collective-permute-start | bytes 344072
  293.6 228.2 %collective-permute-start.1 = (f32[34,512]{1,0:T(8,128)}, f32[34,512]{1,0:T(8,128)}, u32[]{:S(2)}, u32[]{:S(2)}) collective-permute-start(f32[34,512]{1,0:T(8,128)} %slice.106), channel_id=1, source_target_pairs={{0,2},{1,3},{2,4},{3,5},{4,6},{5,7},{6,8},{7,9},{8,10},{9,11},{10,... | collective-permute-start | bytes 208904
  300.8 8.2 copy-start.11
  300.8 8.2 copy-start.13
  300.8 8.2 copy-start.15
  309.0 211.0 %copy-start.37 = (bf16[16,512]{1,0:T(8,128)(2,1)S(1)}, bf16[16,512]{1,0:T(8,128)(2,1)}, u32[]{:S(2)}) copy-start(bf16[16,512]{1,0:T(8,128)(2,1)} %param.14) | copy-start | bytes 49156
  521.2 490.0 %all-reduce.10.cloned.1.call-start = ((), (), s32[]{:S(2)}) async-start(), calls=%async_computation.1 | async-start | bytes 524288 | tf_op jit(solution)/shard_map/psum | solution.py:14
  (15 other events, 25.4 us)
Sparse Core Ops, SparseCore 0:
  521.3 280.4 all-reduce.7
  804.9 206.1 all-reduce.9
